TPU v7x, 128 devices: a whole 4x4x4 slice. The times are simulated.
128 devices in a mesh: wa: 16 (over z, y_hi, core), an: 8 (over y_lo, x).
Axes of the slice: x: 4, y: 4 (y_hi: 2, y_lo: 2; y = y_hi * 2 + y_lo), z: 4, core: 2. Of those that a mesh axis runs over, the one named last changes fastest.
Arguments:
- mass_field: float32 [64, 256, 128, 256], P(None, 'wa', 'an'), may hold values from -8 to 8
- factor_one: float32 [256, 64], replicated, may hold values from -0.375 to 0.375
- factor_two: float32 [256, 64], P('wa'), may hold values from -0.375 to 0.375
- factor_four: float32 [64, 16], replicated, may hold values from -0.75 to 0.75
Outputs:
- gram: float32 [128, 128], P('an')
All inputs are finite; a program needn't handle non-finite values.
Results may differ from a plain program's by a relative error of at most 0.0001.
Values sent between devices are 32-bit elements; how exact they have to be, the bound alone decides.
No kernel may reach another device: no remote copies, remote signals or barrier semaphores. Data moves between devices by JAX's collectives and lax.ppermute only.
A program may use at most 128 MiB of HBM per device.

v0:
```python
import jax
import jax.numpy as jnp
from jax import lax
from jax.sharding import PartitionSpec as P


def on_device(mass_field, factor_one, factor_two, factor_four):
    highest = lax.Precision.HIGHEST
    species_count, fibre_cells, slab_cells, first_cells = mass_field.shape
    rank_one = factor_one.shape[1]
    rank_two = factor_two.shape[1]
    rank_four = factor_four.shape[1]
    reduced = jnp.dot(factor_four.T, mass_field.reshape(species_count, -1), precision=highest)
    reduced = reduced.reshape(rank_four * fibre_cells * slab_cells, first_cells)
    slab_rows = rank_one // lax.axis_size("wa")
    mixed_rows = jnp.dot(reduced, factor_one, precision=highest)
    mixed_rows = mixed_rows.reshape(rank_four, fibre_cells, slab_cells, rank_one)
    term = jnp.einsum("qjkr,jp->rkqp", mixed_rows, factor_two, precision=highest)
    summed = lax.psum(term.reshape(rank_one, slab_cells, rank_four * rank_two), "wa")
    owned_slab = lax.dynamic_slice_in_dim(summed, lax.axis_index("wa") * slab_rows, slab_rows, 0)
    partial_gram = jnp.einsum(
        "rim,rjm->ij",
        owned_slab,
        lax.all_gather(owned_slab, "an", axis=1, tiled=True),
        precision=highest,
    )
    gram_rows = lax.psum(partial_gram, "wa")
    return gram_rows / (rank_one * rank_two * rank_four)


def solution(mesh):
    in_specs = (P(None, "wa", "an", None), P(), P("wa", None), P())
    out_specs = P("an", None)
    return jax.shard_map(
        on_device, mesh=mesh, in_specs=in_specs, out_specs=out_specs, check_vma=False
    )
```

profile of v0, /device:TPU:1, one launch (start us, length us, event | category | flops | bytes accessed | tf_op | source)
XLA Modules:
  0.0 312.5 jit_solution(3219890865373004460)
XLA Ops:
  6.5 0.0 copy-start
  6.5 0.0 all-reduce.2.cloned.1.call-start
  6.5 22.7 %fusion = f32[16,16,16,256]{3,0,2,1:T(8,128)S(1)} fusion(f32[16,16,256,64]{2,1,0,3:T(8,128)} %bitcast.35, f32[64,16]{0,1:T(8,128)} %param.7), kind=kOutput, calls=%fused_computation | convolution fusion | flops 805306368 | bytes 20975616 | tf_op jit(solution)/shard_map/dot_general | solution.py:13
  29.3 0.0 copy-done
  29.3 0.0 copy-start.1
  29.3 5.6 %fusion.2 = f32[16,16,16,64]{3,1,2,0:T(8,128)S(1)} fusion(f32[16,16,16,256]{3,0,2,1:T(8,128)S(1)} %fusion, f32[256,64]{0,1:T(8,128)S(1)} %copy-done), kind=kOutput, calls=%fused_computation.2 | convolution fusion | flops 805306368 | bytes 5308416 | tf_op jit(solution)/shard_map/dot_general | solution.py:16
  34.9 0.0 copy-done.1
  34.9 13.5 %convolution_bitcast_fusion = f32[64,16,16,64]{3,0,1,2:T(8,128)S(1)} fusion(f32[16,16,16,64]{3,1,2,0:T(8,128)S(1)} %fusion.2, f32[16,64]{1,0:T(8,128)S(1)} %copy-done.1), kind=kOutput, calls=%fused_computation.4 | convolution fusion | flops 201326592 | bytes 5246976 | tf_op jit(solution)/shard_map/qjkr,jp->rkqp/dot_general | solution.py:18
  48.4 8.3 %copy.5 = f32[64,16,16,64]{3,2,1,0:T(8,128)} copy(f32[64,16,16,64]{3,0,1,2:T(8,128)S(1)} %convolution_bitcast_fusion) | data formatting | bytes 8388608 | tf_op jit(solution)/shard_map/qjkr,jp->rkqp/transpose | solution.py:18
  56.7 7.6 %reshape.12 = f32[64,16,1024]{2,1,0:T(8,128)} reshape(f32[64,16,16,64]{3,2,1,0:T(8,128)} %copy.5) | data formatting | bytes 8388608 | tf_op jit(solution)/shard_map/reshape | solution.py:19
  64.3 0.0 all-reduce.2.cloned.1.call-update
  64.4 0.0 all-gather.2.cloned.1.call-start
  64.4 158.7 %all-reduce.2.cloned.1.call-done = f32[64,16,1024]{2,1,0:T(8,128)} async-done(((f32[64,16,1024]{2,1,0:T(8,128)}), f32[64,16,1024]{2,1,0:T(8,128)}) %all-reduce.2.cloned.1.call-update) | async-done | bytes 4194320 | tf_op jit(solution)/shard_map/psum | solution.py:19
  223.1 1.7 constant_dynamic-slice_fusion
  224.8 0.0 all-gather.2.cloned.1.call-update
  224.8 38.1 %all-gather.2.cloned.1.call-done = f32[4,128,1024]{2,1,0:T(8,128)} async-done(((f32[4,16,1024]{2,1,0:T(8,128)}), f32[4,128,1024]{2,1,0:T(8,128)}) %all-gather.2.cloned.1.call-update) | async-done | bytes 2097168 | tf_op jit(solution)/shard_map/all_gather | solution.py:24
  262.9 3.4 %convolution_bitcast_fusion.1 = f32[16,128]{1,0:T(8,128)S(1)} fusion(f32[4,16,1024]{2,1,0:T(8,128)} %constant_dynamic-slice_fusion, f32[4,128,1024]{2,1,0:T(8,128)} %all-gather.2.cloned.1.call-done), kind=kOutput, calls=%fused_computation.5 | convolution fusion | flops 100663296 | bytes 2367488 | tf_op jit(solution)/shard_map/rim,rjm->ij/dot_general | solution.py:21
  266.3 38.7 %psum.15 = f32[16,128]{1,0:T(8,128)S(1)} all-reduce(f32[16,128]{1,0:T(8,128)S(1)} %convolution_bitcast_fusion.1), channel_id=1, replica_groups=mesh['wa'=16,'an'=8] {'wa'}, use_global_device_ids=true, to_apply=%region_1.0 | all-reduce | flops 2048 | bytes 16384 | tf_op jit(solution)/shard_map/psum | solution.py:27
  305.0 0.6 broadcast_multiply_fusion
Async XLA Ops:
  6.5 22.7 %copy-start = (f32[256,64]{0,1:T(8,128)S(1)}, f32[256,64]{0,1:T(8,128)}, u32[]{:S(2)}) copy-start(f32[256,64]{0,1:T(8,128)} %param.5) | copy-start | bytes 196612
  6.5 216.6 %all-reduce.2.cloned.1.call-start = ((), (), s32[]{:S(2)}) async-start(), calls=%async_computation | async-start | bytes 8388608 | tf_op jit(solution)/shard_map/psum | solution.py:19
  29.3 5.6 %copy-start.1 = (f32[16,64]{1,0:T(8,128)S(1)}, f32[16,64]{1,0:T(8,128)}, u32[]{:S(2)}) copy-start(f32[16,64]{1,0:T(8,128)} %param.6) | copy-start | bytes 12292
  64.4 198.5 %all-gather.2.cloned.1.call-start = ((), (), s32[]{:S(2)}) async-start(), calls=%async_computation.1 | async-start | bytes 2359296 | tf_op jit(solution)/shard_map/all_gather | solution.py:24
Sparse Core Ops, SparseCore 0:
  64.5 158.5 all-reduce.1
  224.9 37.9 all-gather.1
where the time goes:
time: 313 us; the launch traced here: 312 us
  waiting for transfers between devices  197 us (63%)
  matrix products  45.2 us (14%)
  blocking collectives  38.7 us (12%)
  local copies, waits for them, and re-layouts  17.6 us (6%)
  between operations  13.5 us (4%)
    psum x1, waiting for transfers between devices, on_device(): lax.psum(term.reshape(rank_one, slab_cells, rank_four * rank_two), 'wa')  159 us
    psum x1, blocking collectives, on_device(): gram_rows = lax.psum(partial_gram, 'wa')  38.7 us
    all_gather x1, waiting for transfers between devices, on_device(): lax.all_gather(owned_slab, 'an', axis=1, tiled=True)  38.1 us
    dot_general x1, matrix products, on_device(): jnp.dot(factor_four.T, mass_field.reshape(species_count, -1), precision=h...  22.7 us
    dot_general x1, matrix products, on_device(): jnp.einsum('qjkr,jp->rkqp', mixed_rows, factor_two, precision=highest)  13.5 us
    transpose x1, local copies, waits for them, and re-layouts, on_device(): jnp.einsum('qjkr,jp->rkqp', mixed_rows, factor_two, precision=highest)  8.34 us
    reshape x1, local copies, waits for them, and re-layouts, on_device(): term.reshape(rank_one, slab_cells, rank_four * rank_two)  7.61 us
  transfers between devices with their start and end apart: 2, of which 2 were waited for; matrix products, arithmetic and copies ran while one was open for 0% of the time, Pallas kernels for 0%

commit v1 on v0

--- a/solution.py
+++ b/solution.py
@@ -1,7 +1,15 @@
+import functools
 import jax
 import jax.numpy as jnp
 from jax import lax
 from jax.sharding import PartitionSpec as P
+
+
+def render_the_orders(point, a_name):
+    return lax.all_gather(point, axis_name=a_name).sum(axis=0)
+
+
+solve_sums_all_on_mesh = functools.partial(render_the_orders, a_name="wa")
 
 
 def on_device(mass_field, factor_one, factor_two, factor_four):
@@ -24,7 +32,7 @@
         lax.all_gather(owned_slab, "an", axis=1, tiled=True),
         precision=highest,
     )
-    gram_rows = lax.psum(partial_gram, "wa")
+    gram_rows = solve_sums_all_on_mesh(partial_gram)
     return gram_rows / (rank_one * rank_two * rank_four)
 
 

time: 313 us -> 304 us (0.971)
  blocking collectives: 38.7 us -> 30.1 us
    psum x1 -> x0, blocking collectives: 38.7 us -> none  [on_device(): gram_rows = lax.psum(partial_gram, 'wa')]
    all_gather x0 -> x1, blocking collectives: none -> 30.1 us  [render_the_orders(): return lax.all_gather(point, axis_name=a_name).sum(axis=0)]
where the time goes in v1:
time: 304 us
  waiting for transfers between devices  197 us (65%)
  matrix products  45.2 us (15%)
  blocking collectives  30.1 us (10%)
  local copies, waits for them, and re-layouts  17.6 us (6%)
  between operations  13.5 us (4%)
    psum x1, waiting for transfers between devices, on_device(): lax.psum(term.reshape(rank_one, slab_cells, rank_four * rank_two), 'wa')  159 us
    all_gather x1, waiting for transfers between devices, on_device(): lax.all_gather(owned_slab, 'an', axis=1, tiled=True)  38.1 us
    all_gather x1, blocking collectives, render_the_orders(): return lax.all_gather(point, axis_name=a_name).sum(axis=0)  30.1 us
    dot_general x1, matrix products, on_device(): jnp.dot(factor_four.T, mass_field.reshape(species_count, -1), precision=h...  22.7 us
    dot_general x1, matrix products, on_device(): jnp.einsum('qjkr,jp->rkqp', mixed_rows, factor_two, precision=highest)  13.5 us
    transpose x1, local copies, waits for them, and re-layouts, on_device(): jnp.einsum('qjkr,jp->rkqp', mixed_rows, factor_two, precision=highest)  8.34 us
    reshape x1, local copies, waits for them, and re-layouts, on_device(): term.reshape(rank_one, slab_cells, rank_four * rank_two)  7.61 us
  transfers between devices with their start and end apart: 2, of which 2 were waited for; matrix products, arithmetic and copies ran while one was open for 0% of the time, Pallas kernels for 0%

profile of v1, /device:TPU:1, one launch (start us, length us, event | category | flops | bytes accessed | tf_op | source)
XLA Modules:
  0.0 303.9 jit_solution(16447354227344661514)
XLA Ops:
  6.5 0.0 copy-start
  6.5 0.0 all-reduce.2.cloned.1.call-start
  6.5 22.7 %fusion = f32[16,16,16,256]{3,0,2,1:T(8,128)S(1)} fusion(f32[16,16,256,64]{2,1,0,3:T(8,128)} %bitcast.36, f32[64,16]{0,1:T(8,128)} %param.7), kind=kOutput, calls=%fused_computation | convolution fusion | flops 805306368 | bytes 20975616 | tf_op jit(solution)/shard_map/dot_general | solution.py:21
  29.3 0.0 copy-done
  29.3 0.0 copy-start.1
  29.3 5.6 %fusion.2 = f32[16,16,16,64]{3,1,2,0:T(8,128)S(1)} fusion(f32[16,16,16,256]{3,0,2,1:T(8,128)S(1)} %fusion, f32[256,64]{0,1:T(8,128)S(1)} %copy-done), kind=kOutput, calls=%fused_computation.2 | convolution fusion | flops 805306368 | bytes 5308416 | tf_op jit(solution)/shard_map/dot_general | solution.py:24
  34.9 0.0 copy-done.1
  34.9 13.5 %convolution_bitcast_fusion = f32[64,16,16,64]{3,0,1,2:T(8,128)S(1)} fusion(f32[16,16,16,64]{3,1,2,0:T(8,128)S(1)} %fusion.2, f32[16,64]{1,0:T(8,128)S(1)} %copy-done.1), kind=kOutput, calls=%fused_computation.4 | convolution fusion | flops 201326592 | bytes 5246976 | tf_op jit(solution)/shard_map/qjkr,jp->rkqp/dot_general | solution.py:26
  48.4 8.3 %copy.5 = f32[64,16,16,64]{3,2,1,0:T(8,128)} copy(f32[64,16,16,64]{3,0,1,2:T(8,128)S(1)} %convolution_bitcast_fusion) | data formatting | bytes 8388608 | tf_op jit(solution)/shard_map/qjkr,jp->rkqp/transpose | solution.py:26
  56.7 7.6 %reshape.12 = f32[64,16,1024]{2,1,0:T(8,128)} reshape(f32[64,16,16,64]{3,2,1,0:T(8,128)} %copy.5) | data formatting | bytes 8388608 | tf_op jit(solution)/shard_map/reshape | solution.py:27
  64.3 0.0 all-reduce.2.cloned.1.call-update
  64.4 0.0 all-gather.3.cloned.1.call-start
  64.4 158.7 %all-reduce.2.cloned.1.call-done = f32[64,16,1024]{2,1,0:T(8,128)} async-done(((f32[64,16,1024]{2,1,0:T(8,128)}), f32[64,16,1024]{2,1,0:T(8,128)}) %all-reduce.2.cloned.1.call-update) | async-done | bytes 4194320 | tf_op jit(solution)/shard_map/psum | solution.py:27
  223.1 1.7 constant_dynamic-slice_fusion
  224.8 0.0 all-gather.3.cloned.1.call-update
  224.8 38.1 %all-gather.3.cloned.1.call-done = f32[4,128,1024]{2,1,0:T(8,128)} async-done(((f32[4,16,1024]{2,1,0:T(8,128)}), f32[4,128,1024]{2,1,0:T(8,128)}) %all-gather.3.cloned.1.call-update) | async-done | bytes 2097168 | tf_op jit(solution)/shard_map/all_gather | solution.py:32
  262.9 3.4 %convolution_bitcast_fusion.1 = f32[16,128]{1,0:T(8,128)S(1)} fusion(f32[4,16,1024]{2,1,0:T(8,128)} %constant_dynamic-slice_fusion, f32[4,128,1024]{2,1,0:T(8,128)} %all-gather.3.cloned.1.call-done), kind=kOutput, calls=%fused_computation.5 | convolution fusion | flops 100663296 | bytes 2367488 | tf_op jit(solution)/shard_map/rim,rjm->ij/dot_general | solution.py:29
  266.3 30.1 %all-gather = f32[256,128]{1,0:T(8,128)S(1)} all-gather(f32[16,128]{1,0:T(8,128)S(1)} %convolution_bitcast_fusion.1), channel_id=2, replica_groups=mesh['wa'=16,'an'=8] {'wa'}, dimensions={0}, use_global_device_ids=true | all-gather | bytes 139264 | tf_op jit(solution)/shard_map/all_gather | solution.py:9
  296.4 0.6 broadcast_multiply_fusion
  (1 shorter events, 0.0 us)
Async XLA Ops:
  6.5 22.7 %copy-start = (f32[256,64]{0,1:T(8,128)S(1)}, f32[256,64]{0,1:T(8,128)}, u32[]{:S(2)}) copy-start(f32[256,64]{0,1:T(8,128)} %param.5) | copy-start | bytes 196612
  6.5 216.6 %all-reduce.2.cloned.1.call-start = ((), (), s32[]{:S(2)}) async-start(), calls=%async_computation | async-start | bytes 8388608 | tf_op jit(solution)/shard_map/psum | solution.py:27
  29.3 5.6 %copy-start.1 = (f32[16,64]{1,0:T(8,128)S(1)}, f32[16,64]{1,0:T(8,128)}, u32[]{:S(2)}) copy-start(f32[16,64]{1,0:T(8,128)} %param.6) | copy-start | bytes 12292
  64.4 198.5 %all-gather.3.cloned.1.call-start = ((), (), s32[]{:S(2)}) async-start(), calls=%async_computation.1 | async-start | bytes 2359296 | tf_op jit(solution)/shard_map/all_gather | solution.py:32
Sparse Core Ops, SparseCore 0:
  64.5 158.5 all-reduce.1
  224.9 37.9 all-gather.2
